TPU v7x, 256 devices: a whole 4x4x8 slice. The times are simulated.
256 devices in a mesh: dp: 8 (over z_hi, x), ctx: 32 (over y, z_lo, core).
Axes of the slice: x: 4, y: 4, z: 8 (z_hi: 2, z_lo: 4; z = z_hi * 4 + z_lo), core: 2. Of those that a mesh axis runs over, the one named last changes fastest.
Arguments:
- y_first: bfloat16 [8, 4096, 1024], P('dp', 'ctx'), may hold values from -6 to 6
- x_second: bfloat16 [8, 4096, 1024], P('dp', 'ctx'), may hold values from -40 to 40
- grad_first: bfloat16 [8, 4096, 1024], P('dp', 'ctx'), may hold values from -6 to 6
- grad_second: bfloat16 [8, 4096, 1024], P('dp', 'ctx'), may hold values from -6 to 6
- w_query: bfloat16 [1024, 1024], P('dp'), may hold values from -0.1875 to 0.1875
- w_key: bfloat16 [1024, 1024], P('dp'), may hold values from -0.1875 to 0.1875
- w_value: bfloat16 [1024, 1024], P('dp'), may hold values from -0.1875 to 0.1875
- w_out: bfloat16 [1024, 1024], P('dp'), may hold values from -0.1875 to 0.1875
Outputs:
- x_first: bfloat16 [8, 4096, 1024], P('dp', 'ctx')
- grad_x_second: bfloat16 [8, 4096, 1024], P('dp', 'ctx')
- grad_query: float32 [1024, 1024], P(('dp', 'ctx'))
- grad_out: float32 [1024, 1024], P(('dp', 'ctx'))
All inputs are finite; a program needn't handle non-finite values.
Results may differ from a plain program's by a relative error of at most 0.012.
The roundings to bfloat16 on the way count: a program that leaves them out, or rounds other values in their place, can miss the bound.
Values may be sent and summed in bfloat16 or wider, within the bound.
No kernel may reach another device: no remote copies, remote signals or barrier semaphores. Data moves between devices by JAX's collectives and lax.ppermute only.
A program may use at most 128 MiB of HBM per device.

v0:
```python
import jax
import jax.numpy as jnp
from jax import lax
from jax.sharding import PartitionSpec as P

HEADS = 8
HEAD_DIM = 128


def prefix(shard, axis, combine, identity):
    size, here = (lax.axis_size(axis), lax.axis_index(axis))
    everything = lax.all_gather(shard, axis)
    start = jnp.broadcast_to(jnp.asarray(identity, shard.dtype), shard.shape)

    def turn(k, before):
        reached = k < here
        new = combine(before, everything[k])
        return jnp.where(reached, new, before)

    return lax.fori_loop(0, size, turn, start)


def carried_in(shard, axis, join, neutral):
    count = lax.axis_size(axis)
    place = lax.axis_index(axis)
    ahead = count - 1 - place
    gathered = lax.all_gather(shard.astype(jnp.bfloat16), axis)
    state = jnp.zeros_like(shard) + jnp.asarray(neutral, shard.dtype)

    def one(turn, state):
        source = count - 1 - turn
        return join(state, lax.dynamic_index_in_dim(gathered, source, 0, False).astype(shard.dtype))

    return lax.fori_loop(0, ahead, one, state)


def add_states(earlier, later):
    return earlier + later


def weight_grads(pairs, factor):
    width = pairs[0][0].shape[1]
    blocks = []
    for left, right in pairs:
        made = lax.dot_general(
            left, right, (((0,), (0,)), ((), ())), preferred_element_type=jnp.float32
        )
        blocks.append(factor * made)
    share = lax.psum_scatter(
        jnp.concatenate(blocks, 1), ("dp", "ctx"), scatter_dimension=0, tiled=True
    )
    return tuple((share[:, index * width : (index + 1) * width] for index in range(len(pairs))))


def on_device(y_first, x_second, grad_first, grad_second, w_query, w_key, w_value, w_out):
    batch, tokens_here, width = y_first.shape
    factor = float(batch * tokens_here * lax.axis_size("dp") * lax.axis_size("ctx")) ** (-0.5)
    full_query, full_key, full_value = (
        lax.all_gather(w_query, "dp", axis=0, tiled=True),
        lax.all_gather(w_key, "dp", axis=0, tiled=True),
        lax.all_gather(w_value, "dp", axis=0, tiled=True),
    )
    full_out = lax.all_gather(w_out, "dp", axis=0, tiled=True)
    second_wide = x_second.astype(jnp.float32)
    inv_rms = lax.rsqrt(jnp.mean(second_wide * second_wide, -1, keepdims=True) + 1e-06)
    normed_wide = second_wide * inv_rms
    normed = normed_wide.astype(jnp.bfloat16)

    def project(weight):
        made = jnp.einsum("btd,df->btf", normed, weight, preferred_element_type=jnp.float32)
        return made.astype(jnp.bfloat16).reshape(batch, tokens_here, HEADS, HEAD_DIM)

    queries = project(full_query)
    key_rows = project(full_key)
    values = project(full_value)
    local_state = jnp.einsum(
        "bthe,bthf->bhef", key_rows, values, preferred_element_type=jnp.float32
    )
    zeros_state = jnp.zeros_like(local_state)
    before = prefix(local_state, "ctx", add_states, zeros_state).astype(jnp.bfloat16)
    causal = jnp.tril(jnp.ones((tokens_here, tokens_here), dtype=bool))
    scores = jnp.einsum("bthe,bshe->bhts", queries, key_rows, preferred_element_type=jnp.float32)
    scores = jnp.where(causal[None, None], scores, 0.0).astype(jnp.bfloat16)
    mixed = jnp.einsum("bhts,bshf->bthf", scores, values, preferred_element_type=jnp.float32)
    mixed = mixed + jnp.einsum(
        "bthe,bhef->bthf", queries, before, preferred_element_type=jnp.float32
    )
    inv_head = lax.rsqrt(jnp.mean(mixed * mixed, -1, keepdims=True) + 1e-06)
    unit = mixed * inv_head
    attn_out = unit.astype(jnp.bfloat16).reshape(batch, tokens_here, width)
    attended = jnp.einsum("btf,fd->btd", attn_out, full_out, preferred_element_type=jnp.float32)
    x_first = (y_first.astype(jnp.float32) - attended).astype(jnp.bfloat16)
    grad_unit = jnp.einsum("btd,fd->btf", grad_first, full_out, preferred_element_type=jnp.float32)
    grad_unit = grad_unit.reshape(batch, tokens_here, HEADS, HEAD_DIM)
    grad_mixed = inv_head * (grad_unit - unit * jnp.mean(grad_unit * unit, -1, keepdims=True))
    grad_mixed = grad_mixed.astype(jnp.bfloat16)
    score_grad = jnp.einsum(
        "bthf,bshf->bhts", grad_mixed, values, preferred_element_type=jnp.float32
    )
    score_grad = jnp.where(causal[None, None], score_grad, 0.0).astype(jnp.bfloat16)
    grad_local = jnp.einsum(
        "bthe,bthf->bhef", queries, grad_mixed, preferred_element_type=jnp.float32
    )
    after_state = carried_in(grad_local, "ctx", add_states, zeros_state).astype(jnp.bfloat16)
    query_grad = jnp.einsum(
        "bhts,bshe->bthe", score_grad, key_rows, preferred_element_type=jnp.float32
    )
    query_grad = query_grad + jnp.einsum(
        "bthf,bhef->bthe", grad_mixed, before, preferred_element_type=jnp.float32
    )
    key_grad = jnp.einsum(
        "bhts,bthe->bshe", score_grad, queries, preferred_element_type=jnp.float32
    )
    key_grad = key_grad + jnp.einsum(
        "bshf,bhef->bshe", values, after_state, preferred_element_type=jnp.float32
    )
    value_grad = jnp.einsum(
        "bhts,bthf->bshf", scores, grad_mixed, preferred_element_type=jnp.float32
    )
    value_grad = value_grad + jnp.einsum(
        "bshe,bhef->bshf", key_rows, after_state, preferred_element_type=jnp.float32
    )
    query_grad = query_grad.astype(jnp.bfloat16).reshape(batch, tokens_here, width)
    key_grad = key_grad.astype(jnp.bfloat16).reshape(batch, tokens_here, width)
    value_grad = value_grad.astype(jnp.bfloat16).reshape(batch, tokens_here, width)
    grad_normed = jnp.einsum(
        "btf,df->btd", query_grad, full_query, preferred_element_type=jnp.float32
    )
    grad_normed = grad_normed + jnp.einsum(
        "btf,df->btd", key_grad, full_key, preferred_element_type=jnp.float32
    )
    grad_normed = grad_normed + jnp.einsum(
        "btf,df->btd", value_grad, full_value, preferred_element_type=jnp.float32
    )
    back = inv_rms * (
        grad_normed - normed_wide * jnp.mean(grad_normed * normed_wide, -1, keepdims=True)
    )
    grad_x_second = (grad_second.astype(jnp.float32) + back).astype(jnp.bfloat16)
    pairs = (
        (normed.reshape(-1, width), query_grad.reshape(-1, width)),
        (attn_out.reshape(-1, width), grad_first.reshape(-1, width)),
    )
    grad_query, grad_out = weight_grads(pairs, factor)
    return (x_first, grad_x_second, grad_query, grad_out)


def solution(mesh):
    placed = (
        P("dp", "ctx", None),
        P("dp", "ctx", None),
        P("dp", "ctx", None),
        P("dp", "ctx", None),
        P("dp", None),
        P("dp", None),
        P("dp", None),
        P("dp", None),
    )
    return jax.shard_map(
        on_device,
        mesh=mesh,
        in_specs=placed,
        out_specs=(
            P("dp", "ctx", None),
            P("dp", "ctx", None),
            P(("dp", "ctx"), None),
            P(("dp", "ctx"), None),
        ),
        check_vma=False,
    )
```

profile of v0, /device:TPU:1, one launch (start us, length us, event | category | flops | bytes accessed | tf_op | source)
XLA Modules:
  0.0 815.4 jit_solution(6239691303570350264)
XLA Ops:
  9.5 1.1 fusion.18
  10.6 77.0 %all-gather.13.cloned.1.call-done = bf16[1024,1024]{1,0:T(8,128)(2,1)} async-done(((bf16[128,1024]{1,0:T(8,128)(2,1)}), bf16[1024,1024]{1,0:T(8,128)(2,1)}) %all-gather.13.cloned.1.call-update) | async-done | bytes 2097168 | tf_op jit(solution)/shard_map/all_gather | solution.py:60
  87.5 2.2 convolution_convert_fusion.1
  90.0 71.8 %all-gather.9.cloned.1.call-done = bf16[1024,1024]{1,0:T(8,128)(2,1)} async-done(((bf16[128,1024]{1,0:T(8,128)(2,1)}), bf16[1024,1024]{1,0:T(8,128)(2,1)}) %all-gather.9.cloned.1.call-update) | async-done | bytes 2097168 | tf_op jit(solution)/shard_map/all_gather | solution.py:61
  161.8 2.1 fusion.9
  165.6 70.5 %all-gather.11.cloned.1.call-done = bf16[1024,1024]{1,0:T(8,128)(2,1)} async-done(((bf16[128,1024]{1,0:T(8,128)(2,1)}), bf16[1024,1024]{1,0:T(8,128)(2,1)}) %all-gather.11.cloned.1.call-update) | async-done | bytes 2097168 | tf_op jit(solution)/shard_map/all_gather | solution.py:59
  236.1 2.1 convolution_convert_fusion.2
  239.1 97.4 %all-gather.17.cloned.1.call-done = f32[256,128,128]{2,1,0:T(8,128)} async-done(((f32[8,128,128]{2,1,0:T(8,128)}), f32[256,128,128]{2,1,0:T(8,128)}) %all-gather.17.cloned.1.call-update) | async-done | bytes 16777232 | tf_op jit(solution)/shard_map/all_gather | solution.py:12
  336.5 40.0 %while.27 = (s32[]{:T(128)}, f32[1,8,128,128]{3,2,1,0:T(8,128)S(1)}, s32[]{:T(128)}, f32[32,1,8,128,128]{4,3,2,1,0:T(8,128)}, s32[]{:T(128)}, /*index=5*/s32[]{:T(128)}) while((s32[]{:T(128)}, f32[1,8,128,128]{3,2,1,0:T(8,128)S(1)}, s32[]{:T(128)}, f32[32,1,8,128,128]{4,3,2,1,0:T(8,128)}, s32[]{:T(128)}, /*index=5*/s32[]{:T(128)}) %tuple.88), condition=%wide.region_2.3_spmd.clone, body=%wide.region_1.2_spmd.clone.sunk | while | flops 393220 | bytes 1572965 | solution.py:20
  336.5 1.2 add_select_fusion.2
  337.7 1.2 add_select_fusion.2
  339.0 1.2 add_select_fusion.2
  340.2 1.2 add_select_fusion.2
  341.5 1.2 add_select_fusion.2
  342.7 1.2 add_select_fusion.2
  344.0 1.2 add_select_fusion.2
  345.2 1.2 add_select_fusion.2
  346.5 1.2 add_select_fusion.2
  347.7 1.2 add_select_fusion.2
  349.0 1.2 add_select_fusion.2
  350.2 1.2 add_select_fusion.2
  351.5 1.2 add_select_fusion.2
  352.8 1.2 add_select_fusion.2
  354.0 1.2 add_select_fusion.2
  355.3 1.2 add_select_fusion.2
  356.5 1.2 add_select_fusion.2
  357.8 1.2 add_select_fusion.2
  359.0 1.2 add_select_fusion.2
  360.3 1.2 add_select_fusion.2
  361.5 1.2 add_select_fusion.2
  362.8 1.2 add_select_fusion.2
  364.0 1.2 add_select_fusion.2
  365.3 1.2 add_select_fusion.2
  366.5 1.2 add_select_fusion.2
  367.8 1.2 add_select_fusion.2
  369.0 1.2 add_select_fusion.2
  370.3 1.2 add_select_fusion.2
  371.6 1.2 add_select_fusion.2
  372.8 1.2 add_select_fusion.2
  374.1 1.2 add_select_fusion.2
  375.3 1.2 add_select_fusion.2
  376.8 35.7 %all-gather.15.cloned.1.call-done = bf16[1024,1024]{1,0:T(8,128)(2,1)} async-done(((bf16[128,1024]{1,0:T(8,128)(2,1)}), bf16[1024,1024]{1,0:T(8,128)(2,1)}) %all-gather.15.cloned.1.call-update) | async-done | bytes 2097168 | tf_op jit(solution)/shard_map/all_gather | solution.py:63
  412.5 2.3 multiply_reduce_fusion
  418.1 4.1 pad_maximum_fusion
  424.4 2.1 fusion.53
  426.5 1.8 fusion.51
  428.3 1.2 fusion.5
  429.5 269.7 %all-reduce.3.cloned.1.call-done = f32[1024,2048]{0,1:T(8,128)} async-done(((f32[1024,2048]{0,1:T(8,128)}), f32[1024,2048]{0,1:T(8,128)}) %all-reduce.3.cloned.1.call-update) | async-done | bytes 8388624
  699.2 1.5 fusion.49
  702.3 68.8 %all-gather.19.cloned.1.call-done = bf16[256,128,128]{2,1,0:T(8,128)(2,1)} async-done(((bf16[8,128,128]{2,1,0:T(8,128)(2,1)}), bf16[256,128,128]{2,1,0:T(8,128)(2,1)}) %all-gather.19.cloned.1.call-update) | async-done | bytes 8388624 | tf_op jit(solution)/shard_map/all_gather | solution.py:27
  771.2 32.9 %while.26 = (s32[]{:T(128)}, f32[1,8,128,128]{3,2,1,0:T(8,128)S(1)}, s32[]{:T(128)}, bf16[32,1,8,128,128]{4,3,2,1,0:T(8,128)(2,1)}, s32[]{:T(128)}, /*index=5*/s32[]{:T(128)}, s32[]{:T(128)}, s32[]{:T(128)}) while((s32[]{:T(128)}, f32[1,8,128,128]{3,2,1,0:T(8,128)S(1)}, s32[]{:T(128)}, bf16[32,1,8,128,128]{4,3,2,1,0:T(8,128)(2,1)}, s32[]{:T(128)}, ...), condition=%wide.region_6.7_spmd, body=%wide.region_5.6_spmd.sunk | while | flops 262150 | bytes 1310863 | solution.py:34
  771.3 1.2 convert_add_fusion.2
  772.4 1.1 convert_add_fusion.2
  773.5 1.1 convert_add_fusion.2
  775.7 1.1 convert_add_fusion.2
  776.8 1.1 convert_add_fusion.2
  777.9 1.1 convert_add_fusion.2
  780.1 1.1 convert_add_fusion.2
  781.2 1.1 convert_add_fusion.2
  782.3 1.1 convert_add_fusion.2
  784.5 1.1 convert_add_fusion.2
  785.6 1.1 convert_add_fusion.2
  788.8 1.1 convert_add_fusion.2
  789.9 1.1 convert_add_fusion.2
  (98 shorter events, 34.8 us)
Async XLA Ops:
  7.2 405.4 %copy-start = (bf16[1,128,1024]{2,1,0:T(8,128)(2,1)S(1)}, bf16[1,128,1024]{2,1,0:T(8,128)(2,1)}, u32[]{:S(2)}) copy-start(bf16[1,128,1024]{2,1,0:T(8,128)(2,1)} %param.14) | copy-start | bytes 786436
  7.2 80.4 %all-gather.13.cloned.1.call-start = ((), (), s32[]{:S(2)}) async-start(), calls=%async_computation.2 | async-start | bytes 2359296 | tf_op jit(solution)/shard_map/all_gather | solution.py:60
  7.9 153.9 %all-gather.9.cloned.1.call-start = ((), (), s32[]{:S(2)}) async-start(), calls=%async_computation | async-start | bytes 2359296 | tf_op jit(solution)/shard_map/all_gather | solution.py:61
  8.7 153.2 %copy-start.2 = (bf16[1,128,1024]{2,1,0:T(8,128)(2,1)S(1)}, bf16[1,128,1024]{2,1,0:T(8,128)(2,1)}, u32[]{:S(2)}) copy-start(bf16[1,128,1024]{2,1,0:T(8,128)(2,1)} %param.13) | copy-start | bytes 786436
  8.7 227.4 %all-gather.11.cloned.1.call-start = ((), (), s32[]{:S(2)}) async-start(), calls=%async_computation.1 | async-start | bytes 2359296 | tf_op jit(solution)/shard_map/all_gather | solution.py:59
  9.4 327.1 %all-gather.17.cloned.1.call-start = ((), (), s32[]{:S(2)}) async-start(), calls=%async_computation.4 | async-start | bytes 17301504 | tf_op jit(solution)/shard_map/all_gather | solution.py:12
  89.7 148.7 %copy-start.10 = (bf16[128,1024]{1,0:T(8,128)(2,1)}, bf16[128,1024]{1,0:T(8,128)(2,1)S(1)}, u32[]{:S(2)}) copy-start(bf16[128,1024]{1,0:T(8,128)(2,1)S(1)} %convolution_convert_fusion.1) | copy-start | bytes 786436
  165.0 247.6 %all-gather.15.cloned.1.call-start = ((), (), s32[]{:S(2)}) async-start(), calls=%async_computation.3 | async-start | bytes 2359296 | tf_op jit(solution)/shard_map/all_gather | solution.py:63
  165.6 533.6 %all-reduce.3.cloned.1.call-start = ((), (), s32[]{:S(2)}) async-start(), calls=%async_computation.6 | async-start | bytes 16777216
  238.7 97.8 %copy-start.14 = (bf16[8,128,128]{2,1,0:T(8,128)(2,1)}, bf16[8,128,128]{2,1,0:T(8,128)(2,1)S(1)}, u32[]{:S(2)}) copy-start(bf16[8,128,128]{2,1,0:T(8,128)(2,1)S(1)} %fusion.3) | copy-start | bytes 786436
  415.0 2.3 copy-start.7
  415.4 0.7 copy-start.15
  416.6 5.7 copy-start.9
  422.2 1.1 copy-start.16
  422.3 4.3 copy-start.5
  422.3 348.9 %all-gather.19.cloned.1.call-start = ((), (), s32[]{:S(2)}) async-start(), calls=%async_computation.5 | async-start | bytes 8650752 | tf_op jit(solution)/shard_map/all_gather | solution.py:27
  424.4 3.9 copy-start.6
  424.4 3.9 copy-start.8
  424.4 3.9 copy-start.18
  771.2 32.9 %copy-start.12 = (f32[8,128,128]{2,1,0:T(8,128)S(1)}, f32[8,128,128]{2,1,0:T(8,128)}, u32[]{:S(2)}) copy-start(f32[8,128,128]{2,1,0:T(8,128)} %fusion.52) | copy-start | bytes 1572868
  771.2 33.2 %copy-start.11 = (bf16[128,1024]{1,0:T(8,128)(2,1)S(1)}, bf16[128,1024]{1,0:T(8,128)(2,1)}, u32[]{:S(2)}) copy-start(bf16[128,1024]{1,0:T(8,128)(2,1)} %copy-done.10) | copy-start | bytes 786436
  771.2 33.2 %copy-start.13 = (f32[8,128,128]{2,1,0:T(8,128)S(1)}, f32[8,128,128]{2,1,0:T(8,128)}, u32[]{:S(2)}) copy-start(f32[8,128,128]{2,1,0:T(8,128)} %fusion.53) | copy-start | bytes 1572868
  804.1 1.6 copy-start.3
  804.8 1.8 copy-start.4
  806.5 1.0 copy-start.17
  806.6 2.0 copy-start.1
Sparse Core Ops, SparseCore 0:
  10.6 76.8 all-gather.12
  90.2 71.6 all-gather.8
  164.5 71.6 all-gather.10
  237.8 98.6 all-gather.16
  339.0 73.5 all-gather.14
  422.4 276.7 all-reduce.2
  701.1 70.0 all-gather.18
where the time goes:
time: 818 us; the launch traced here: 815 us
  waiting for transfers between devices  694 us (85%)
  other arithmetic  77.8 us (10%)
  matrix products  22.5 us (3%)
  between operations  14.5 us (2%)
    unnamed x8, waiting for transfers between devices  272 us
    all_gather x1, waiting for transfers between devices, prefix(): everything = lax.all_gather(shard, axis)  97.4 us
    all_gather x1, waiting for transfers between devices, on_device(): lax.all_gather(w_key, 'dp', axis=0, tiled=True)  77 us
    all_gather x1, waiting for transfers between devices, on_device(): lax.all_gather(w_value, 'dp', axis=0, tiled=True)  71.8 us
    all_gather x1, waiting for transfers between devices, on_device(): lax.all_gather(w_query, 'dp', axis=0, tiled=True)  70.5 us
    all_gather x1, waiting for transfers between devices, carried_in(): gathered = lax.all_gather(shard.astype(jnp.bfloat16), axis)  68.8 us
    select_n x32, other arithmetic, turn(): return jnp.where(reached, new, before)  39.3 us
    all_gather x1, waiting for transfers between devices, on_device(): full_out = lax.all_gather(w_out, 'dp', axis=0, tiled=True)  35.7 us
  transfers between devices with their start and end apart: 7, of which 7 were waited for; matrix products, arithmetic and copies ran while one was open for 7% of the time, Pallas kernels for 0%

commit v1 on v0

--- a/solution.py
+++ b/solution.py
@@ -5,6 +5,18 @@
 
 HEADS = 8
 HEAD_DIM = 128
+
+
+def follow_surface(local, across, which_dim):
+    return jnp.concatenate(
+        jax.lax.all_to_all(
+            jnp.stack([local for _ in range(jax.lax.axis_size(across))]),
+            across,
+            split_axis=0,
+            concat_axis=0,
+        ),
+        axis=which_dim,
+    )
 
 
 def prefix(shard, axis, combine, identity):
@@ -58,7 +70,7 @@
     full_query, full_key, full_value = (
         lax.all_gather(w_query, "dp", axis=0, tiled=True),
         lax.all_gather(w_key, "dp", axis=0, tiled=True),
-        lax.all_gather(w_value, "dp", axis=0, tiled=True),
+        follow_surface(w_value, "dp", 0),
     )
     full_out = lax.all_gather(w_out, "dp", axis=0, tiled=True)
     second_wide = x_second.astype(jnp.float32)

time: 818 us -> 775 us (0.947)
  waiting for transfers between devices: 694 us -> 625 us
  starting transfers between devices: 0.27 us -> 11.8 us
    all_gather x1 -> x0, waiting for transfers between devices: 71.8 us -> none  [on_device(): lax.all_gather(w_value, 'dp', axis=0, tiled=True)]
    all_gather x1, waiting for transfers between devices: 77 us -> 94.1 us  [on_device(): lax.all_gather(w_key, 'dp', axis=0, tiled=True)]
    all_to_all x0 -> x1, starting transfers between devices: none -> 11.6 us  [follow_surface(): jax.lax.all_to_all(jnp.stack([local for _ in range(jax.lax.axis_size(acro...]
    unnamed x8 -> x7, waiting for transfers between devices: 272 us -> 269 us
  transfers between devices with their start and end apart: 7 -> 7, of which waited for: 7 -> 6; matrix products, arithmetic and copies ran while one was open for 7% -> 9% of each run, Pallas kernels for 0% -> 0%
where the time goes in v1:
time: 775 us; the launch traced here: 772 us
  waiting for transfers between devices  625 us (81%)
  other arithmetic  76.8 us (10%)
  matrix products  29.7 us (4%)
  between operations  14.5 us (2%)
  local copies, waits for them, and re-layouts  12.1 us (2%)
  starting transfers between devices  11.8 us (2%)
    unnamed x7, waiting for transfers between devices  269 us
    all_gather x1, waiting for transfers between devices, on_device(): lax.all_gather(w_key, 'dp', axis=0, tiled=True)  94.1 us
    all_gather x1, waiting for transfers between devices, prefix(): everything = lax.all_gather(shard, axis)  92.5 us
    all_gather x1, waiting for transfers between devices, on_device(): lax.all_gather(w_query, 'dp', axis=0, tiled=True)  68.3 us
    all_gather x1, waiting for transfers between devices, carried_in(): gathered = lax.all_gather(shard.astype(jnp.bfloat16), axis)  66.9 us
    select_n x32, other arithmetic, turn(): return jnp.where(reached, new, before)  39.3 us
    all_gather x1, waiting for transfers between devices, on_device(): full_out = lax.all_gather(w_out, 'dp', axis=0, tiled=True)  33.9 us
    add x30, other arithmetic, add_states(): return earlier + later  32.1 us
  transfers between devices with their start and end apart: 7, of which 6 were waited for; matrix products, arithmetic and copies ran while one was open for 9% of the time, Pallas kernels for 0%

profile of v1, /device:TPU:1, one launch (start us, length us, event | category | flops | bytes accessed | tf_op | source)
XLA Modules:
  0.0 771.5 jit_solution(11877163302674368486)
XLA Ops:
  7.9 2.6 stack.2
  10.5 11.6 %all-to-all-start = ((bf16[8,128,1024]{2,1,0:T(8,128)(2,1)}), bf16[8,128,1024]{2,1,0:T(8,128)(2,1)S(1)}, u32[]{:S(2)}, u32[]{:S(2)}) async-start(bf16[8,128,1024]{2,1,0:T(8,128)(2,1)} %stack.2), calls=%async_computation | async-start | bytes 4194304 | tf_op jit(solution)/shard_map/all_to_all | solution.py:12
  23.0 94.1 %all-gather.10.cloned.1.call-done = bf16[1024,1024]{1,0:T(8,128)(2,1)} async-done(((bf16[128,1024]{1,0:T(8,128)(2,1)}), bf16[1024,1024]{1,0:T(8,128)(2,1)}) %all-gather.10.cloned.1.call-update) | async-done | bytes 2097168 | tf_op jit(solution)/shard_map/all_gather | solution.py:72
  117.1 2.1 convolution_convert_fusion.1
  123.1 68.3 %all-gather.8.cloned.1.call-done = bf16[1024,1024]{1,0:T(8,128)(2,1)} async-done(((bf16[128,1024]{1,0:T(8,128)(2,1)}), bf16[1024,1024]{1,0:T(8,128)(2,1)}) %all-gather.8.cloned.1.call-update) | async-done | bytes 2097168 | tf_op jit(solution)/shard_map/all_gather | solution.py:71
  191.4 2.8 convolution_convert_fusion.2
  194.2 1.1 copy.61
  195.3 1.3 fusion.3
  197.3 2.1 fusion.23
  199.4 92.5 %all-gather.14.cloned.1.call-done = f32[256,128,128]{2,1,0:T(8,128)} async-done(((f32[8,128,128]{2,1,0:T(8,128)}), f32[256,128,128]{2,1,0:T(8,128)}) %all-gather.14.cloned.1.call-update) | async-done | bytes 16777232 | tf_op jit(solution)/shard_map/all_gather | solution.py:24
  291.9 40.0 %while.27 = (s32[]{:T(128)}, f32[1,8,128,128]{3,2,1,0:T(8,128)S(1)}, s32[]{:T(128)}, f32[32,1,8,128,128]{4,3,2,1,0:T(8,128)}, s32[]{:T(128)}, /*index=5*/s32[]{:T(128)}) while((s32[]{:T(128)}, f32[1,8,128,128]{3,2,1,0:T(8,128)S(1)}, s32[]{:T(128)}, f32[32,1,8,128,128]{4,3,2,1,0:T(8,128)}, s32[]{:T(128)}, /*index=5*/s32[]{:T(128)}) %tuple.86), condition=%wide.region_2.3_spmd.clone, body=%wide.region_1.2_spmd.clone.sunk | while | flops 393220 | bytes 1572965 | solution.py:32
  291.9 1.2 add_select_fusion.2
  293.2 1.2 add_select_fusion.2
  294.4 1.2 add_select_fusion.2
  295.7 1.2 add_select_fusion.2
  296.9 1.2 add_select_fusion.2
  298.2 1.2 add_select_fusion.2
  299.4 1.2 add_select_fusion.2
  300.7 1.2 add_select_fusion.2
  301.9 1.2 add_select_fusion.2
  303.2 1.2 add_select_fusion.2
  304.4 1.2 add_select_fusion.2
  305.7 1.2 add_select_fusion.2
  306.9 1.2 add_select_fusion.2
  308.2 1.2 add_select_fusion.2
  309.4 1.2 add_select_fusion.2
  310.7 1.2 add_select_fusion.2
  311.9 1.2 add_select_fusion.2
  313.2 1.2 add_select_fusion.2
  314.4 1.2 add_select_fusion.2
  315.7 1.2 add_select_fusion.2
  317.0 1.2 add_select_fusion.2
  318.2 1.2 add_select_fusion.2
  319.5 1.2 add_select_fusion.2
  320.7 1.2 add_select_fusion.2
  322.0 1.2 add_select_fusion.2
  323.2 1.2 add_select_fusion.2
  324.5 1.2 add_select_fusion.2
  325.7 1.2 add_select_fusion.2
  327.0 1.2 add_select_fusion.2
  328.2 1.2 add_select_fusion.2
  329.5 1.2 add_select_fusion.2
  330.7 1.2 add_select_fusion.2
  332.0 2.1 multiply_reduce_fusion.1
  334.1 33.9 %all-gather.12.cloned.1.call-done = bf16[1024,1024]{1,0:T(8,128)(2,1)} async-done(((bf16[128,1024]{1,0:T(8,128)(2,1)}), bf16[1024,1024]{1,0:T(8,128)(2,1)}) %all-gather.12.cloned.1.call-update) | async-done | bytes 2097168 | tf_op jit(solution)/shard_map/all_gather | solution.py:75
  368.0 2.5 multiply_reduce_fusion
  373.3 4.1 pad_maximum_fusion
  379.4 2.0 fusion.52
  382.4 3.2 fusion.51
  385.6 1.2 fusion.5
  386.8 267.5 %all-reduce.3.cloned.1.call-done = f32[1024,2048]{0,1:T(8,128)} async-done(((f32[1024,2048]{0,1:T(8,128)}), f32[1024,2048]{0,1:T(8,128)}) %all-reduce.3.cloned.1.call-update) | async-done | bytes 8388624
  654.3 2.3 fusion.49
  656.6 1.8 copy.52
  659.2 66.9 %all-gather.16.cloned.1.call-done = bf16[256,128,128]{2,1,0:T(8,128)(2,1)} async-done(((bf16[8,128,128]{2,1,0:T(8,128)(2,1)}), bf16[256,128,128]{2,1,0:T(8,128)(2,1)}) %all-gather.16.cloned.1.call-update) | async-done | bytes 8388624 | tf_op jit(solution)/shard_map/all_gather | solution.py:39
  726.2 32.8 %while.26 = (s32[]{:T(128)}, f32[1,8,128,128]{3,2,1,0:T(8,128)S(1)}, s32[]{:T(128)}, bf16[32,1,8,128,128]{4,3,2,1,0:T(8,128)(2,1)}, s32[]{:T(128)}, /*index=5*/s32[]{:T(128)}, s32[]{:T(128)}, s32[]{:T(128)}) while((s32[]{:T(128)}, f32[1,8,128,128]{3,2,1,0:T(8,128)S(1)}, s32[]{:T(128)}, bf16[32,1,8,128,128]{4,3,2,1,0:T(8,128)(2,1)}, s32[]{:T(128)}, ...), condition=%wide.region_6.7_spmd, body=%wide.region_5.6_spmd.sunk | while | flops 262150 | bytes 1310863 | solution.py:46
  726.2 1.1 convert_add_fusion.2
  727.3 1.1 convert_add_fusion.2
  728.4 1.1 convert_add_fusion.2
  730.6 1.1 convert_add_fusion.2
  731.7 1.1 convert_add_fusion.2
  732.8 1.1 convert_add_fusion.2
  735.0 1.1 convert_add_fusion.2
  759.0 1.5 fusion.7
  760.5 1.4 fusion.8
  (110 shorter events, 40.0 us)
Async XLA Ops:
  7.2 360.8 %copy-start = (bf16[1,128,1024]{2,1,0:T(8,128)(2,1)S(1)}, bf16[1,128,1024]{2,1,0:T(8,128)(2,1)}, u32[]{:S(2)}) copy-start(bf16[1,128,1024]{2,1,0:T(8,128)(2,1)} %param.14) | copy-start | bytes 786436
  7.2 109.9 %all-gather.10.cloned.1.call-start = ((), (), s32[]{:S(2)}) async-start(), calls=%async_computation.2 | async-start | bytes 2359296 | tf_op jit(solution)/shard_map/all_gather | solution.py:72
  10.5 12.4 %copy-start.2 = (bf16[1,128,1024]{2,1,0:T(8,128)(2,1)S(1)}, bf16[1,128,1024]{2,1,0:T(8,128)(2,1)}, u32[]{:S(2)}) copy-start(bf16[1,128,1024]{2,1,0:T(8,128)(2,1)} %param.13) | copy-start | bytes 786436
  10.5 109.6 %all-to-all-start = ((bf16[8,128,1024]{2,1,0:T(8,128)(2,1)}), bf16[8,128,1024]{2,1,0:T(8,128)(2,1)S(1)}, u32[]{:S(2)}, u32[]{:S(2)}) async-start(bf16[8,128,1024]{2,1,0:T(8,128)(2,1)} %stack.2), calls=%async_computation | async-start | bytes 4194304 | tf_op jit(solution)/shard_map/all_to_all | solution.py:12
  22.1 169.3 %all-gather.8.cloned.1.call-start = ((), (), s32[]{:S(2)}) async-start(), calls=%async_computation.1 | async-start | bytes 2359296 | tf_op jit(solution)/shard_map/all_gather | solution.py:71
  22.8 269.1 %all-gather.14.cloned.1.call-start = ((), (), s32[]{:S(2)}) async-start(), calls=%async_computation.4 | async-start | bytes 17301504 | tf_op jit(solution)/shard_map/all_gather | solution.py:24
  119.2 0.7 copy-start.17
  120.1 2.3 copy-start.11
  120.6 0.7 copy-start.8
  122.4 245.6 %all-gather.12.cloned.1.call-start = ((), (), s32[]{:S(2)}) async-start(), calls=%async_computation.3 | async-start | bytes 2359296 | tf_op jit(solution)/shard_map/all_gather | solution.py:75
  123.0 531.3 %all-reduce.3.cloned.1.call-start = ((), (), s32[]{:S(2)}) async-start(), calls=%async_computation.6 | async-start | bytes 16777216
  196.6 0.7 copy-start.20
  368.0 2.5 copy-start.5
  368.0 2.7 copy-start.9
  368.0 3.0 copy-start.12
  370.6 0.9 copy-start.6
  370.6 1.8 copy-start.13
  371.0 0.7 copy-start.22
  371.5 1.0 copy-start.15
  377.4 0.9 copy-start.7
  377.4 3.9 copy-start.21
  377.4 4.9 copy-start.16
  377.4 348.7 %all-gather.16.cloned.1.call-start = ((), (), s32[]{:S(2)}) async-start(), calls=%async_computation.5 | async-start | bytes 8650752 | tf_op jit(solution)/shard_map/all_gather | solution.py:39
  381.3 4.3 copy-start.4
  381.3 4.3 copy-start.14
  381.3 4.3 copy-start.24
  726.1 32.9 %copy-start.10 = (bf16[16,8,8,128]{3,2,1,0:T(8,128)(2,1)S(1)}, bf16[16,8,8,128]{3,2,1,0:T(8,128)(2,1)}, u32[]{:S(2)}) copy-start(bf16[16,8,8,128]{3,2,1,0:T(8,128)(2,1)} %copy-done.8) | copy-start | bytes 786436
  726.1 34.4 %copy-start.18 = (bf16[128,1024]{1,0:T(8,128)(2,1)S(1)}, bf16[128,1024]{1,0:T(8,128)(2,1)}, u32[]{:S(2)}) copy-start(bf16[128,1024]{1,0:T(8,128)(2,1)} %copy-done.17) | copy-start | bytes 786436
  759.0 2.9 copy-start.3
  759.0 2.9 copy-start.19
  762.7 1.0 copy-start.23
  762.8 1.9 copy-start.1
Sparse Core Ops, SparseCore 0:
  10.6 106.4 all-gather.9
  119.7 71.6 all-gather.7
  193.2 98.6 all-gather.13
  294.4 73.5 all-gather.11
  377.5 276.6 all-reduce.2
  656.0 70.0 all-gather.15
